TPU v7x, 512 devices: a whole 4x8x8 slice. The times are simulated.
512 devices in a mesh: seq: 128 (over y, z, core), head: 4 (over x).
Axes of the slice: x: 4, y: 8, z: 8, core: 2. Of those that a mesh axis runs over, the one named last changes fastest.
Arguments:
- out_grad: bfloat16 [16384, 4096], P('seq', 'head'), may hold values from -6 to 6
- expert_ids: int32 [16384, 8], P('seq'), may hold values from 0 to 127, all different within a row; in each aligned block of 128 rows (0 to 127, 128 to 255, ...) at most 12 rows name the same one
- top_logits: float32 [16384, 8], P('seq'), may hold values from -10 to 310
- doc_start: int32 [16384], P('seq'), may hold values from 0 to 16383, as said below
- router: bfloat16 [128, 4096], P(None, 'head'), may hold values from -0.09375 to 0.09375
- w_down: bfloat16 [128, 768, 4096], P('seq', None, 'head'), may hold values from -0.21875 to 0.21875
- saved_gu: bfloat16 [128, 2, 768, 1536], P('seq', None, 'head'), may hold values from -6 to 6
- out_weight: bfloat16 [4096, 4096], P('head', 'seq'), may hold values from -0.09375 to 0.09375
- query: bfloat16 [16384, 32, 128], P('seq', 'head'), may hold values from -64 to 64
- key: bfloat16 [16384, 4, 128], P('seq', 'head'), may hold values from -8 to 8
- value: bfloat16 [16384, 4, 128], P('seq', 'head'), may hold values from -6 to 6
Outputs:
- gate_up_grad: bfloat16 [128, 2, 768, 1536], P('seq', None, 'head')
- route_grad: float32 [16384, 8], P('seq')
- query_grad: bfloat16 [16384, 32, 128], P('seq', 'head')
- key_grad: bfloat16 [16384, 4, 128], P('seq', 'head')
- value_grad: bfloat16 [16384, 4, 128], P('seq', 'head')
Inputs may be any that keep to these rules, and one draw needn't show every extreme that they name: `expert_ids`: each token names 8 different experts; among the 128 tokens of one index of seq no expert is named by more than 12 tokens. doc_start[t] is the first position of the document that holds t; documents lie end to end, each has at most 896 tokens and one has exactly 896.
All inputs are finite; a program needn't handle non-finite values.
Results may differ from a plain program's by a relative error of at most 0.03.
Values may be sent and summed in bfloat16 or wider, within the bound.
No kernel may reach another device: no remote copies, remote signals or barrier semaphores. Data moves between devices by JAX's collectives and lax.ppermute only.
A program may use at most 128 MiB of HBM per device.

v0:
```python
import jax
import jax.numpy as jnp
from jax import lax
from jax.sharding import PartitionSpec as P

REACH = 7
masked_score = -1e30
highest = lax.Precision.HIGHEST


def passed_along(array, axis, by):
    count = lax.axis_size(axis)
    pairs = [(i, i + by) for i in range(count) if 0 <= i + by < count]
    return lax.ppermute(array, axis, pairs)


def attend(queries, upstream, keys_all, values_all, query_pos, key_pos, doc_begin, score_scale):
    scores = (
        jnp.einsum("tkgd,lkd->kgtl", queries, keys_all, preferred_element_type=jnp.float32)
        * score_scale
    )
    valid = (key_pos[None, :] <= query_pos[:, None]) & (key_pos[None, :] >= doc_begin[:, None])
    scores = jnp.where(valid[None, None], scores, masked_score)
    row_max = jnp.max(scores, axis=3, keepdims=True)
    exponent = jnp.exp(scores - row_max)
    probs = exponent / jnp.sum(exponent, axis=3, keepdims=True)
    dprob = jnp.einsum("tkgd,lkd->kgtl", upstream, values_all, preferred_element_type=jnp.float32)
    row_dot = jnp.sum(probs * dprob, axis=3, keepdims=True)
    probs_b = probs.astype(jnp.bfloat16)
    dscore = (probs * (dprob - row_dot)).astype(jnp.bfloat16)
    query_part = (
        jnp.einsum("kgtl,lkd->tkgd", dscore, keys_all, preferred_element_type=jnp.float32)
        * score_scale
    )
    key_part = (
        jnp.einsum("kgtl,tkgd->lkd", dscore, queries, preferred_element_type=jnp.float32)
        * score_scale
    )
    value_part = jnp.einsum("kgtl,tkgd->lkd", probs_b, upstream, preferred_element_type=jnp.float32)
    return (query_part, key_part, value_part)


def per_device(
    out_grad,
    expert_ids,
    top_logits,
    doc_start,
    router,
    w_down,
    saved_gu,
    out_weight,
    query,
    key,
    value,
):
    seq_count = lax.axis_size("seq")
    seq_index = lax.axis_index("seq")
    tokens_here = out_grad.shape[0]
    features = out_grad.shape[1]
    slots_all = saved_gu.shape[3]
    capacity = slots_all // seq_count
    experts = router.shape[0]
    top_count = expert_ids.shape[1]
    weights = jax.nn.softmax(top_logits, axis=1)
    hits = (expert_ids[:, :, None] == jnp.arange(experts, dtype=jnp.int32)[None, None, :]).astype(
        jnp.float32
    )
    per_token = jnp.sum(hits, axis=1)
    earlier = (jnp.arange(tokens_here)[:, None] > jnp.arange(tokens_here)[None, :]).astype(
        jnp.float32
    )
    before = jnp.dot(earlier, per_token, precision=highest)
    rank = jnp.sum(hits * before[:, None, :], axis=2).astype(jnp.int32)
    target = expert_ids * capacity + rank
    placed = (
        target[None, :, :] == jnp.arange(experts * capacity, dtype=jnp.int32)[:, None, None]
    ).astype(jnp.float32)
    pick = jnp.sum(placed, axis=2).astype(jnp.bfloat16)
    send_rows = jnp.dot(pick, out_grad, preferred_element_type=jnp.float32).astype(jnp.bfloat16)
    send_weight = jnp.sum(placed * weights[None, :, :], axis=(1, 2)).astype(jnp.bfloat16)
    weight_lanes = jnp.zeros((experts * capacity, 128), jnp.bfloat16).at[:, 0].set(send_weight)
    payload = jnp.concatenate([send_rows, weight_lanes], axis=1)
    weight_full = out_weight
    kv_heads = key.shape[1]
    head_dim = key.shape[2]
    group = query.shape[1] // kv_heads
    paired = jnp.stack([key, value])
    blocks = [paired]
    for distance in range(1, REACH + 1):
        blocks.append(passed_along(paired, "seq", distance))
    sent_payload = lax.all_to_all(
        payload.reshape(experts, capacity, features + 128),
        "seq",
        split_axis=0,
        concat_axis=0,
        tiled=True,
    ).reshape(slots_all, features + 128)
    sent_payload, weight_full, blocks = lax.optimization_barrier(
        (sent_payload, weight_full, tuple(blocks))
    )
    slot_rows = sent_payload[:, :features]
    sent_weight = sent_payload[:, features]
    weight_here = w_down[0]
    raw = lax.psum_scatter(
        lax.dot_general(
            weight_here, slot_rows, (((1,), (1,)), ((), ())), preferred_element_type=jnp.float32
        ).astype(jnp.bfloat16),
        "head",
        scatter_dimension=0,
        tiled=True,
    ).astype(jnp.float32)
    gate = saved_gu[0, 0].astype(jnp.float32)
    up = saved_gu[0, 1].astype(jnp.float32)
    sig = jax.nn.sigmoid(gate)
    act = gate * sig
    hidden = act * up
    slot_part = jnp.sum(hidden * raw, axis=0)
    scaled = raw * sent_weight.reshape(slots_all).astype(jnp.float32)[None, :]
    gate_up_grad = jnp.stack([scaled * up * sig * (1.0 + gate * (1.0 - sig)), scaled * act])[
        None
    ].astype(jnp.bfloat16)
    slot_grad = lax.psum(slot_part, "head")
    returned = lax.all_to_all(
        slot_grad.reshape(seq_count, capacity), "seq", split_axis=0, concat_axis=0, tiled=True
    )
    route_grad = jnp.take(returned.reshape(-1), target.reshape(-1)).reshape(tokens_here, top_count)
    logit_grad = weights * (route_grad - jnp.sum(weights * route_grad, axis=1, keepdims=True))
    dense = jnp.einsum("tk,tke->te", logit_grad, hits, precision=highest)
    router_term = jnp.dot(dense, router.astype(jnp.float32), precision=highest)
    input_slice = (out_grad.astype(jnp.float32) + router_term).astype(jnp.bfloat16)
    input_grad = lax.all_gather(input_slice, "head", axis=1, tiled=True)
    core = seq_index % 2
    by_parity = input_grad.reshape(tokens_here, seq_count // 2, 2, -1)
    mine = lax.dynamic_index_in_dim(by_parity, core, axis=2, keepdims=False)
    theirs = lax.dynamic_index_in_dim(by_parity, 1 - core, axis=2, keepdims=False)
    ordered = jnp.concatenate(
        [mine.reshape(tokens_here, -1), theirs.reshape(tokens_here, -1)], axis=1
    )
    attn_grad = lax.dot_general(
        ordered, weight_full, (((1,), (1,)), ((), ())), preferred_element_type=jnp.float32
    ).astype(jnp.bfloat16)
    window = jnp.concatenate(blocks[::-1], axis=1)
    local_pos = jnp.arange(tokens_here, dtype=jnp.int32)
    key_pos = jnp.concatenate(
        [(seq_index - distance) * tokens_here + local_pos for distance in range(REACH, -1, -1)]
    )
    query_pos = seq_index * tokens_here + local_pos
    queries = query.reshape(tokens_here, kv_heads, group, head_dim)
    upstream = attn_grad.reshape(tokens_here, kv_heads, group, head_dim)
    query_part, key_part, value_part = attend(
        queries, upstream, window[0], window[1], query_pos, key_pos, doc_start, head_dim ** (-0.5)
    )
    query_grad = query_part.reshape(query.shape).astype(jnp.bfloat16)
    pieces = jnp.stack([key_part, value_part]).reshape(
        2, REACH + 1, tokens_here, kv_heads, head_dim
    )
    totals = pieces[:, REACH]
    for distance in range(1, REACH + 1):
        totals = totals + passed_along(
            pieces[:, REACH - distance].astype(jnp.bfloat16), "seq", -distance
        ).astype(jnp.float32)
    return (
        gate_up_grad,
        route_grad,
        query_grad,
        totals[0].astype(jnp.bfloat16),
        totals[1].astype(jnp.bfloat16),
    )


def gather_columns(out_weight):
    half = lax.all_gather(out_weight, "chip", axis=1, tiled=True)
    other = lax.ppermute(half, "core", [(0, 1), (1, 0)])
    return jnp.concatenate([half, other], axis=1)


def solution(mesh):
    chips = mesh.devices.shape[0] // 2
    split_mesh = jax.sharding.Mesh(
        mesh.devices.reshape(chips, 2, mesh.devices.shape[1]), ("chip", "core", "head")
    )
    gather = jax.shard_map(
        gather_columns,
        mesh=split_mesh,
        in_specs=P("head", ("chip", "core")),
        out_specs=P("head", ("chip", "core")),
        check_vma=False,
    )
    in_specs = (
        P("seq", "head"),
        P("seq", None),
        P("seq", None),
        P("seq"),
        P(None, "head"),
        P("seq", None, "head"),
        P("seq", None, "head", None),
        P("head", "seq"),
        P("seq", "head", None),
        P("seq", "head", None),
        P("seq", "head", None),
    )
    out_specs = (
        P("seq", None, "head", None),
        P("seq", None),
        P("seq", "head", None),
        P("seq", "head", None),
        P("seq", "head", None),
    )
    body = jax.shard_map(
        per_device, mesh=mesh, in_specs=in_specs, out_specs=out_specs, check_vma=False
    )

    def run(*args):
        args = list(args)
        args[7] = gather(args[7])
        return body(*args)

    return run
```

profile of v0, /device:TPU:49, one launch (start us, length us, event | category | flops | bytes accessed | tf_op | source)
XLA Modules:
  0.0 424.8 jit_solution(11453210561158346732)
XLA Ops:
  13.0 11.6 %convert_reduce_fusion = (bf16[1536,128]{1,0:T(8,128)(2,1)S(1)}, bf16[1536]{0:T(1024)(128)(2,1)S(1)}) fusion(s32[128,8]{0,1:T(8,128)S(1)} %convert_add_fusion, f32[128,8]{0,1:T(8,128)S(1)} %fusion.55), kind=kLoop, calls=%fused_computation.5 | loop fusion | flops 7666176 | bytes 404480 | tf_op jit(solution)/shard_map/reduce_sum | solution.py:78
  29.3 5.8 %copy.130 = bf16[1536,1152]{1,0:T(8,128)(2,1)} copy(bf16[1536,1152]{0,1:T(8,128)(2,1)} %fusion.6) | data formatting | bytes 7077888 | tf_op jit(solution)/shard_map/concatenate | solution.py:82
  35.1 6.5 %reshape.406 = bf16[128,12,1152]{2,1,0:T(8,128)(2,1)} reshape(bf16[1536,1152]{1,0:T(8,128)(2,1)} %copy.130) | data formatting | bytes 7077888 | tf_op jit(solution)/shard_map/reshape | solution.py:92
  41.6 18.2 %all-to-all-start = ((bf16[128,12,1152]{2,1,0:T(8,128)(2,1)}), bf16[128,12,1152]{2,1,0:T(8,128)(2,1)}, u32[]{:S(2)}, u32[]{:S(2)}) async-start(bf16[128,12,1152]{2,1,0:T(8,128)(2,1)} %reshape.406), calls=%async_computation | async-start | bytes 9437184 | tf_op jit(solution)/shard_map/all_to_all | solution.py:91
  59.8 135.4 %all-gather.3.cloned.1.call-done = bf16[1024,2048]{0,1:T(8,128)(2,1)} async-done(((bf16[1024,32]{0,1:T(8,128)(2,1)}), bf16[1024,2048]{0,1:T(8,128)(2,1)}) %all-gather.3.cloned.1.call-update) | async-done | bytes 4194320 | tf_op jit(solution)/shard_map/all_gather | solution.py:172
  195.2 5.7 %collective-permute-start = (bf16[1024,2048]{0,1:T(8,128)(2,1)}, bf16[1024,2048]{0,1:T(8,128)(2,1)}, u32[]{:S(2)}, u32[]{:S(2)}) collective-permute-start(bf16[1024,2048]{0,1:T(8,128)(2,1)} %all-gather.3.cloned.1.call-done), channel_id=1, source_target_pairs={{0,4},{4,0},{1,5},{5,1},{2,6},{6,2},{3,7},{7,3},{8,12},{12,8},{9,1... | collective-permute-start | bytes 12582920 | tf_op jit(solution)/shard_map/ppermute | solution.py:173
  205.5 3.6 collective-permute-start.3
  212.4 6.6 %reshape.407 = bf16[1536,1152]{1,0:T(8,128)(2,1)} reshape(bf16[128,12,1152]{2,1,0:T(8,128)(2,1)} %all-to-all-done) | data formatting | bytes 7077888 | tf_op jit(solution)/shard_map/reshape | solution.py:97
  219.0 5.4 %collective-permute-start.5 = (bf16[2,128,1,128]{3,1,2,0:T(8,128)(2,1)S(1)}, bf16[2,128,1,128]{3,1,2,0:T(8,128)(2,1)S(1)}, u32[]{:S(2)}, u32[]{:S(2)}) collective-permute-start(bf16[2,128,1,128]{3,1,2,0:T(8,128)(2,1)S(1)} %pad_maximum_fusion.3), channel_id=1, source_target_pairs={{0,20},{4,24},{8,28},{12,32},{16,36},{20,40},{24,44},{28,48},{32,5... | collective-permute-start | bytes 196616 | tf_op jit(solution)/shard_map/ppermute | solution.py:14
  226.4 7.1 %collective-permute-start.7 = (bf16[2,128,1,128]{3,1,2,0:T(8,128)(2,1)S(1)}, bf16[2,128,1,128]{3,1,2,0:T(8,128)(2,1)S(1)}, u32[]{:S(2)}, u32[]{:S(2)}) collective-permute-start(bf16[2,128,1,128]{3,1,2,0:T(8,128)(2,1)S(1)} %pad_maximum_fusion.3), channel_id=1, source_target_pairs={{0,28},{4,32},{8,36},{12,40},{16,44},{20,48},{24,52},{28,56},{32,6... | collective-permute-start | bytes 196616 | tf_op jit(solution)/shard_map/ppermute | solution.py:14
  233.5 7.7 %pad_maximum_fusion = bf16[1024,4096]{0,1:T(8,128)(2,1)} fusion(bf16[1024,2048]{0,1:T(8,128)(2,1)} %collective-permute-done, bf16[1024,2048]{0,1:T(8,128)(2,1)} %all-gather.3.cloned.1.call-done), kind=kLoop, calls=%fused_computation.1 | loop fusion | flops 16777216 | bytes 16777216 | tf_op jit(solution)/shard_map/concatenate | solution.py:174
  241.3 6.0 %fusion.9 = bf16[768,1536]{0,1:T(8,128)(2,1)} fusion(bf16[1536,1152]{1,0:T(8,128)(2,1)} %reshape.407, bf16[1,768,1024]{2,1,0:T(8,128)(2,1)S(1)} %copy-done), kind=kOutput, calls=%fused_computation.21 | convolution fusion | flops 2417098752 | bytes 7077888 | tf_op jit(solution)/shard_map/dot_general | solution.py:105
  247.3 4.4 %copy.154 = bf16[768,1536]{1,0:T(8,128)(2,1)} copy(bf16[768,1536]{0,1:T(8,128)(2,1)} %fusion.9) | data formatting | bytes 4718592
  254.8 30.1 %reduce-scatter.4.cloned.1.call-done = bf16[192,1536]{1,0:T(8,128)(2,1)} async-done(((bf16[768,1536]{1,0:T(8,128)(2,1)}), bf16[192,1536]{1,0:T(8,128)(2,1)}) %reduce-scatter.4.cloned.1.call-update) | async-done | bytes 589840
  288.8 12.9 %psum.7 = f32[128,1,12]{2,0,1:T(8,128)} all-reduce(f32[128,1,12]{2,0,1:T(8,128)S(1)} %all_to_all.10), channel_id=1, replica_groups=mesh['chip'=64,'core'=2,'head'=4] {'head'}, use_global_device_ids=true, to_apply=%region_9.0 | all-reduce | flops 1536 | bytes 12288 | tf_op jit(solution)/shard_map/psum | solution.py:122
  301.8 18.3 %all-to-all-start.1 = ((f32[128,1,12]{2,1,0:T(1,128)}), f32[128,1,12]{2,1,0:T(1,128)S(1)}, u32[]{:S(2)}, u32[]{:S(2)}) async-start(f32[128,1,12]{2,1,0:T(1,128)} %bitcast.10), calls=%async_computation.1 | async-start | bytes 131072 | tf_op jit(solution)/shard_map/all_to_all | solution.py:123
  320.4 7.9 %all-to-all-done.1 = f32[128,1,12]{2,1,0:T(1,128)S(1)} async-done(((f32[128,1,12]{2,1,0:T(1,128)}), f32[128,1,12]{2,1,0:T(1,128)S(1)}, u32[]{:S(2)}, u32[]{:S(2)}) %all-to-all-start.1) | async-done | bytes 6176 | tf_op jit(solution)/shard_map/all_to_all | solution.py:123
  329.8 6.2 %gather_fusion = f32[1024]{0:T(1024)S(1)} fusion(f32[1536]{0:T(1024)S(1)} %reshape.408, s32[1024]{0:T(1024)S(1)} %broadcast_clamp_fusion), kind=kCustom, calls=%fused_computation | custom fusion | bytes 12288 | tf_op jit(solution)/shard_map/jit(_take)/gather | solution.py:126
  341.9 17.5 %all-gather.5.cloned.1.call-done = bf16[128,4096]{1,0:T(8,128)(2,1)} async-done(((bf16[128,1024]{1,0:T(8,128)(2,1)}), bf16[128,4096]{1,0:T(8,128)(2,1)}) %all-gather.5.cloned.1.call-update) | async-done | bytes 1048592 | tf_op jit(solution)/shard_map/all_gather | solution.py:131
  361.2 4.8 %convolution_convert_fusion.2 = bf16[128,1024]{1,0:T(8,128)(2,1)S(1)} fusion(bf16[1024,4096]{0,1:T(8,128)(2,1)} %pad_maximum_fusion, bf16[128,2048]{0,1:T(8,128)(2,1)S(1)} %bitcast.183, bf16[128,2048]{0,1:T(8,128)(2,1)S(1)} %bitcast.182), kind=kOutput, calls=%fused_computation.51 | convolution fusion | flops 1075970048 | bytes 9699328 | tf_op jit(solution)/shard_map/dot_general | solution.py:139
  370.8 4.2 copy.142
  380.6 9.3 %collective-permute-start.14 = (bf16[2,128,1,128]{3,1,2,0:T(8,128)(2,1)}, bf16[2,128,1,128]{3,1,2,0:T(8,128)(2,1)}, u32[]{:S(2)}, u32[]{:S(2)}) collective-permute-start(bf16[2,128,1,128]{3,1,2,0:T(8,128)(2,1)} %get-tuple-element.82), channel_id=1, source_target_pairs={{28,0},{32,4},{36,8},{40,12},{44,16},{48,20},{52,24},{56,28},{60,3... | collective-permute-start | bytes 196616 | tf_op jit(solution)/shard_map/ppermute | solution.py:14
  395.8 5.2 %collective-permute-start.12 = (bf16[2,128,1,128]{3,1,0,2:T(8,128)(2,1)S(1)}, bf16[2,128,1,128]{3,1,0,2:T(8,128)(2,1)S(1)}, u32[]{:S(2)}, u32[]{:S(2)}) collective-permute-start(bf16[2,128,1,128]{3,1,0,2:T(8,128)(2,1)S(1)} %get-tuple-element.84), channel_id=1, source_target_pairs={{20,0},{24,4},{28,8},{32,12},{36,16},{40,20},{44,24},{48,28},{52,3... | collective-permute-start | bytes 196616 | tf_op jit(solution)/shard_map/ppermute | solution.py:14
  404.6 4.4 %collective-permute-start.10 = (bf16[2,128,1,128]{3,1,0,2:T(8,128)(2,1)S(1)}, bf16[2,128,1,128]{3,1,0,2:T(8,128)(2,1)S(1)}, u32[]{:S(2)}, u32[]{:S(2)}) collective-permute-start(bf16[2,128,1,128]{3,1,0,2:T(8,128)(2,1)S(1)} %get-tuple-element.86), channel_id=1, source_target_pairs={{12,0},{16,4},{20,8},{24,12},{28,16},{32,20},{36,24},{40,28},{44,3... | collective-permute-start | bytes 196616 | tf_op jit(solution)/shard_map/ppermute | solution.py:14
  (160 shorter events, 65.2 us)
Async XLA Ops:
  7.2 234.1 %copy-start = (bf16[1,768,1024]{2,1,0:T(8,128)(2,1)S(1)}, bf16[1,768,1024]{2,1,0:T(8,128)(2,1)}, u32[]{:S(2)}) copy-start(bf16[1,768,1024]{2,1,0:T(8,128)(2,1)} %param.19) | copy-start | bytes 4718596
  7.2 188.0 %all-gather.3.cloned.1.call-start = ((), (), s32[]{:S(2)}) async-start(), calls=%async_computation.3 | async-start | bytes 4259840 | tf_op jit(solution)/shard_map/all_gather | solution.py:172
  41.6 159.4 %copy-start.26 = (bf16[128,1,128]{2,0,1:T(8,128)(2,1)S(1)}, bf16[128,1,128]{2,0,1:T(8,128)(2,1)}, u32[]{:S(2)}) copy-start(bf16[128,1,128]{2,0,1:T(8,128)(2,1)} %param.24) | copy-start | bytes 98308
  41.6 159.4 %copy-start.27 = (bf16[128,1,128]{2,0,1:T(8,128)(2,1)S(1)}, bf16[128,1,128]{2,0,1:T(8,128)(2,1)}, u32[]{:S(2)}) copy-start(bf16[128,1,128]{2,0,1:T(8,128)(2,1)} %param.23) | copy-start | bytes 98308
  41.6 170.8 %all-to-all-start = ((bf16[128,12,1152]{2,1,0:T(8,128)(2,1)}), bf16[128,12,1152]{2,1,0:T(8,128)(2,1)}, u32[]{:S(2)}, u32[]{:S(2)}) async-start(bf16[128,12,1152]{2,1,0:T(8,128)(2,1)} %reshape.406), calls=%async_computation | async-start | bytes 9437184 | tf_op jit(solution)/shard_map/all_to_all | solution.py:91
  59.7 225.1 %reduce-scatter.4.cloned.1.call-start = ((), (), s32[]{:S(2)}) async-start(), calls=%async_computation.5 | async-start | bytes 2949120
  195.2 31.2 %collective-permute-start = (bf16[1024,2048]{0,1:T(8,128)(2,1)}, bf16[1024,2048]{0,1:T(8,128)(2,1)}, u32[]{:S(2)}, u32[]{:S(2)}) collective-permute-start(bf16[1024,2048]{0,1:T(8,128)(2,1)} %all-gather.3.cloned.1.call-done), channel_id=1, source_target_pairs={{0,4},{4,0},{1,5},{5,1},{2,6},{6,2},{3,7},{7,3},{8,12},{12,8},{9,1... | collective-permute-start | bytes 12582920 | tf_op jit(solution)/shard_map/ppermute | solution.py:173
  201.0 18.1 %collective-permute-start.1 = (bf16[2,128,1,128]{3,1,2,0:T(8,128)(2,1)S(1)}, bf16[2,128,1,128]{3,1,2,0:T(8,128)(2,1)S(1)}, u32[]{:S(2)}, u32[]{:S(2)}) collective-permute-start(bf16[2,128,1,128]{3,1,2,0:T(8,128)(2,1)S(1)} %pad_maximum_fusion.3), channel_id=1, source_target_pairs={{0,4},{4,8},{8,12},{12,16},{16,20},{20,24},{24,28},{28,32},{32,36}... | collective-permute-start | bytes 196616 | tf_op jit(solution)/shard_map/ppermute | solution.py:14
  203.5 21.0 %collective-permute-start.2 = (bf16[2,128,1,128]{3,1,2,0:T(8,128)(2,1)S(1)}, bf16[2,128,1,128]{3,1,2,0:T(8,128)(2,1)S(1)}, u32[]{:S(2)}, u32[]{:S(2)}) collective-permute-start(bf16[2,128,1,128]{3,1,2,0:T(8,128)(2,1)S(1)} %pad_maximum_fusion.3), channel_id=1, source_target_pairs={{0,8},{4,12},{8,16},{12,20},{16,24},{20,28},{24,32},{28,36},{32,40... | collective-permute-start | bytes 196616 | tf_op jit(solution)/shard_map/ppermute | solution.py:14
  205.5 35.7 %collective-permute-start.3 = (bf16[2,128,1,128]{3,1,2,0:T(8,128)(2,1)S(1)}, bf16[2,128,1,128]{3,1,2,0:T(8,128)(2,1)S(1)}, u32[]{:S(2)}, u32[]{:S(2)}) collective-permute-start(bf16[2,128,1,128]{3,1,2,0:T(8,128)(2,1)S(1)} %pad_maximum_fusion.3), channel_id=1, source_target_pairs={{0,12},{4,16},{8,20},{12,24},{16,28},{20,32},{24,36},{28,40},{32,4... | collective-permute-start | bytes 196616 | tf_op jit(solution)/shard_map/ppermute | solution.py:14
  209.2 32.0 %collective-permute-start.4 = (bf16[2,128,1,128]{3,1,2,0:T(8,128)(2,1)S(1)}, bf16[2,128,1,128]{3,1,2,0:T(8,128)(2,1)S(1)}, u32[]{:S(2)}, u32[]{:S(2)}) collective-permute-start(bf16[2,128,1,128]{3,1,2,0:T(8,128)(2,1)S(1)} %pad_maximum_fusion.3), channel_id=1, source_target_pairs={{0,16},{4,20},{8,24},{12,28},{16,32},{20,36},{24,40},{28,44},{32,4... | collective-permute-start | bytes 196616 | tf_op jit(solution)/shard_map/ppermute | solution.py:14
  219.0 22.2 %collective-permute-start.5 = (bf16[2,128,1,128]{3,1,2,0:T(8,128)(2,1)S(1)}, bf16[2,128,1,128]{3,1,2,0:T(8,128)(2,1)S(1)}, u32[]{:S(2)}, u32[]{:S(2)}) collective-permute-start(bf16[2,128,1,128]{3,1,2,0:T(8,128)(2,1)S(1)} %pad_maximum_fusion.3), channel_id=1, source_target_pairs={{0,20},{4,24},{8,28},{12,32},{16,36},{20,40},{24,44},{28,48},{32,5... | collective-permute-start | bytes 196616 | tf_op jit(solution)/shard_map/ppermute | solution.py:14
  224.5 16.7 %collective-permute-start.6 = (bf16[2,128,1,128]{3,1,2,0:T(8,128)(2,1)S(1)}, bf16[2,128,1,128]{3,1,2,0:T(8,128)(2,1)S(1)}, u32[]{:S(2)}, u32[]{:S(2)}) collective-permute-start(bf16[2,128,1,128]{3,1,2,0:T(8,128)(2,1)S(1)} %pad_maximum_fusion.3), channel_id=1, source_target_pairs={{0,24},{4,28},{8,32},{12,36},{16,40},{20,44},{24,48},{28,52},{32,5... | collective-permute-start | bytes 196616 | tf_op jit(solution)/shard_map/ppermute | solution.py:14
  226.4 14.8 %collective-permute-start.7 = (bf16[2,128,1,128]{3,1,2,0:T(8,128)(2,1)S(1)}, bf16[2,128,1,128]{3,1,2,0:T(8,128)(2,1)S(1)}, u32[]{:S(2)}, u32[]{:S(2)}) collective-permute-start(bf16[2,128,1,128]{3,1,2,0:T(8,128)(2,1)S(1)} %pad_maximum_fusion.3), channel_id=1, source_target_pairs={{0,28},{4,32},{8,36},{12,40},{16,44},{20,48},{24,52},{28,56},{32,6... | collective-permute-start | bytes 196616 | tf_op jit(solution)/shard_map/ppermute | solution.py:14
  286.2 50.6 %copy-start.8 = (bf16[128,1024]{1,0:T(8,128)(2,1)S(1)}, bf16[128,1024]{1,0:T(8,128)(2,1)}, u32[]{:S(2)}) copy-start(bf16[128,1024]{1,0:T(8,128)(2,1)} %param.14) | copy-start | bytes 786436
  301.8 26.6 %all-to-all-start.1 = ((f32[128,1,12]{2,1,0:T(1,128)}), f32[128,1,12]{2,1,0:T(1,128)S(1)}, u32[]{:S(2)}, u32[]{:S(2)}) async-start(f32[128,1,12]{2,1,0:T(1,128)} %bitcast.10), calls=%async_computation.1 | async-start | bytes 131072 | tf_op jit(solution)/shard_map/all_to_all | solution.py:123
  320.1 39.3 %all-gather.5.cloned.1.call-start = ((), (), s32[]{:S(2)}) async-start(), calls=%async_computation.4 | async-start | bytes 1310720 | tf_op jit(solution)/shard_map/all_gather | solution.py:131
  380.6 28.4 %collective-permute-start.14 = (bf16[2,128,1,128]{3,1,2,0:T(8,128)(2,1)}, bf16[2,128,1,128]{3,1,2,0:T(8,128)(2,1)}, u32[]{:S(2)}, u32[]{:S(2)}) collective-permute-start(bf16[2,128,1,128]{3,1,2,0:T(8,128)(2,1)} %get-tuple-element.82), channel_id=1, source_target_pairs={{28,0},{32,4},{36,8},{40,12},{44,16},{48,20},{52,24},{56,28},{60,3... | collective-permute-start | bytes 196616 | tf_op jit(solution)/shard_map/ppermute | solution.py:14
  390.0 21.1 %collective-permute-start.13 = (bf16[2,128,1,128]{3,1,0,2:T(8,128)(2,1)S(1)}, bf16[2,128,1,128]{3,1,0,2:T(8,128)(2,1)}, u32[]{:S(2)}, u32[]{:S(2)}) collective-permute-start(bf16[2,128,1,128]{3,1,0,2:T(8,128)(2,1)S(1)} %get-tuple-element.83), channel_id=1, source_target_pairs={{24,0},{28,4},{32,8},{36,12},{40,16},{44,20},{48,24},{52,28},{56,3... | collective-permute-start | bytes 196616 | tf_op jit(solution)/shard_map/ppermute | solution.py:14
  395.8 20.5 %collective-permute-start.12 = (bf16[2,128,1,128]{3,1,0,2:T(8,128)(2,1)S(1)}, bf16[2,128,1,128]{3,1,0,2:T(8,128)(2,1)S(1)}, u32[]{:S(2)}, u32[]{:S(2)}) collective-permute-start(bf16[2,128,1,128]{3,1,0,2:T(8,128)(2,1)S(1)} %get-tuple-element.84), channel_id=1, source_target_pairs={{20,0},{24,4},{28,8},{32,12},{36,16},{40,20},{44,24},{48,28},{52,3... | collective-permute-start | bytes 196616 | tf_op jit(solution)/shard_map/ppermute | solution.py:14
  401.0 15.3 %collective-permute-start.11 = (bf16[2,128,1,128]{3,1,0,2:T(8,128)(2,1)S(1)}, bf16[2,128,1,128]{3,1,0,2:T(8,128)(2,1)S(1)}, u32[]{:S(2)}, u32[]{:S(2)}) collective-permute-start(bf16[2,128,1,128]{3,1,0,2:T(8,128)(2,1)S(1)} %get-tuple-element.85), channel_id=1, source_target_pairs={{16,0},{20,4},{24,8},{28,12},{32,16},{36,20},{40,24},{44,28},{48,3... | collective-permute-start | bytes 196616 | tf_op jit(solution)/shard_map/ppermute | solution.py:14
  404.6 11.7 %collective-permute-start.10 = (bf16[2,128,1,128]{3,1,0,2:T(8,128)(2,1)S(1)}, bf16[2,128,1,128]{3,1,0,2:T(8,128)(2,1)S(1)}, u32[]{:S(2)}, u32[]{:S(2)}) collective-permute-start(bf16[2,128,1,128]{3,1,0,2:T(8,128)(2,1)S(1)} %get-tuple-element.86), channel_id=1, source_target_pairs={{12,0},{16,4},{20,8},{24,12},{28,16},{32,20},{36,24},{40,28},{44,3... | collective-permute-start | bytes 196616 | tf_op jit(solution)/shard_map/ppermute | solution.py:14
  409.0 7.3 %collective-permute-start.9 = (bf16[2,128,1,128]{3,1,0,2:T(8,128)(2,1)S(1)}, bf16[2,128,1,128]{3,1,0,2:T(8,128)(2,1)S(1)}, u32[]{:S(2)}, u32[]{:S(2)}) collective-permute-start(bf16[2,128,1,128]{3,1,0,2:T(8,128)(2,1)S(1)} %get-tuple-element.87), channel_id=1, source_target_pairs={{8,0},{12,4},{16,8},{20,12},{24,16},{28,20},{32,24},{36,28},{40,32... | collective-permute-start | bytes 196616 | tf_op jit(solution)/shard_map/ppermute | solution.py:14
  411.1 5.6 %collective-permute-start.8 = (bf16[2,128,1,128]{3,1,0,2:T(8,128)(2,1)S(1)}, bf16[2,128,1,128]{3,1,0,2:T(8,128)(2,1)S(1)}, u32[]{:S(2)}, u32[]{:S(2)}) collective-permute-start(bf16[2,128,1,128]{3,1,0,2:T(8,128)(2,1)S(1)} %get-tuple-element.81), channel_id=1, source_target_pairs={{4,0},{8,4},{12,8},{16,12},{20,16},{24,20},{28,24},{32,28},{36,32}... | collective-permute-start | bytes 196616 | tf_op jit(solution)/shard_map/ppermute | solution.py:14
  (25 other events, 663.4 us)
Sparse Core Ops, SparseCore 0:
  11.0 184.1 all-gather.2
  251.8 32.9 reduce-scatter.3
  338.1 21.2 all-gather.4
where the time goes:
time: 427 us; the launch traced here: 425 us
  waiting for transfers between devices  192 us (45%)
  starting transfers between devices  97.6 us (23%)
  local copies, waits for them, and re-layouts  45.6 us (11%)
  other arithmetic  38.5 us (9%)
  matrix products  23.4 us (5%)
  between operations  14.7 us (3%)
  blocking collectives  12.9 us (3%)
    all_gather x1, waiting for transfers between devices, gather_columns(): half = lax.all_gather(out_weight, 'chip', axis=1, tiled=True)  135 us
    ppermute x14, starting transfers between devices, passed_along(): return lax.ppermute(array, axis, pairs)  55.1 us
    unnamed x4, waiting for transfers between devices  30.8 us
    all_to_all x1, starting transfers between devices, per_device(): lax.all_to_all(slot_grad.reshape(seq_count, capacity), 'seq', split_axis=...  18.3 us
    all_to_all x1, starting transfers between devices, per_device(): lax.all_to_all(payload.reshape(experts, capacity, features + 128), 'seq',...  18.2 us
    all_gather x1, waiting for transfers between devices, per_device(): input_grad = lax.all_gather(input_slice, 'head', axis=1, tiled=True)  17.5 us
    psum x1, blocking collectives, per_device(): slot_grad = lax.psum(slot_part, 'head')  12.9 us
    unnamed x73, local copies, waits for them, and re-layouts  11.7 us
  transfers between devices with their start and end apart: 20, of which 5 were waited for; matrix products, arithmetic and copies ran while one was open for 14% of the time, Pallas kernels for 0%

commit v1 on v0

--- a/solution.py
+++ b/solution.py
@@ -169,7 +169,9 @@
 
 
 def gather_columns(out_weight):
-    half = lax.all_gather(out_weight, "chip", axis=1, tiled=True)
+    half = jnp.concatenate(
+        lax.all_to_all(jnp.stack([out_weight] * lax.axis_size("chip")), "chip", 0, 0), axis=1
+    )
     other = lax.ppermute(half, "core", [(0, 1), (1, 0)])
     return jnp.concatenate([half, other], axis=1)
 

time: 427 us -> 512 us (1.20)
  waiting for transfers between devices: 192 us -> 245 us
  starting transfers between devices: 97.6 us -> 130 us
    all_gather x1 -> x0, waiting for transfers between devices: 135 us -> none  [gather_columns(): half = lax.all_gather(out_weight, 'chip', axis=1, tiled=True)]
    all_to_all x1, waiting for transfers between devices: 0.01 us -> 97.9 us  [per_device(): lax.all_to_all(payload.reshape(experts, capacity, features + 128), 'seq',...]
    all_to_all x0 -> x1, waiting for transfers between devices: none -> 85.3 us  [gather_columns(): lax.all_to_all(jnp.stack([out_weight] * lax.axis_size('chip')), 'chip', 0...]
    all_to_all x1, starting transfers between devices: 18.2 us -> 36.6 us  [per_device(): lax.all_to_all(payload.reshape(experts, capacity, features + 128), 'seq',...]
    all_to_all x0 -> x1, starting transfers between devices: none -> 16 us  [gather_columns(): lax.all_to_all(jnp.stack([out_weight] * lax.axis_size('chip')), 'chip', 0...]
    unnamed x4 -> x3, waiting for transfers between devices: 30.8 us -> 36.1 us
    unnamed x73 -> x81, local copies, waits for them, and re-layouts: 11.7 us -> 11.5 us
  transfers between devices with their start and end apart: 20 -> 20, of which waited for: 5 -> 6; matrix products, arithmetic and copies ran while one was open for 14% -> 11% of each run, Pallas kernels for 0% -> 0%
where the time goes in v1:
time: 512 us; the launch traced here: 510 us
  waiting for transfers between devices  245 us (48%)
  starting transfers between devices  130 us (25%)
  local copies, waits for them, and re-layouts  48.8 us (10%)
  other arithmetic  35.6 us (7%)
  matrix products  22.6 us (4%)
  between operations  15 us (3%)
  blocking collectives  12.9 us (3%)
    all_to_all x1, waiting for transfers between devices, per_device(): lax.all_to_all(payload.reshape(experts, capacity, features + 128), 'seq',...  97.9 us
    all_to_all x1, waiting for transfers between devices, gather_columns(): lax.all_to_all(jnp.stack([out_weight] * lax.axis_size('chip')), 'chip', 0...  85.3 us
    ppermute x14, starting transfers between devices, passed_along(): return lax.ppermute(array, axis, pairs)  56.6 us
    all_to_all x1, starting transfers between devices, per_device(): lax.all_to_all(payload.reshape(experts, capacity, features + 128), 'seq',...  36.6 us
    unnamed x3, waiting for transfers between devices  36.1 us
    all_to_all x1, starting transfers between devices, per_device(): lax.all_to_all(slot_grad.reshape(seq_count, capacity), 'seq', split_axis=...  18.3 us
    all_gather x1, waiting for transfers between devices, per_device(): input_grad = lax.all_gather(input_slice, 'head', axis=1, tiled=True)  17.6 us
    all_to_all x1, starting transfers between devices, gather_columns(): lax.all_to_all(jnp.stack([out_weight] * lax.axis_size('chip')), 'chip', 0...  16 us
  transfers between devices with their start and end apart: 20, of which 6 were waited for; matrix products, arithmetic and copies ran while one was open for 11% of the time, Pallas kernels for 0%

profile of v1, /device:TPU:49, one launch (start us, length us, event | category | flops | bytes accessed | tf_op | source)
XLA Modules:
  0.0 510.3 jit_solution(14820125270549169203)
XLA Ops:
  10.7 16.0 %all-to-all-start = ((bf16[64,1024,32]{1,2,0:T(8,128)(2,1)}), bf16[64,1024,32]{1,2,0:T(8,128)(2,1)}, u32[]{:S(2)}, u32[]{:S(2)}) async-start(bf16[64,1024,32]{1,2,0:T(8,128)(2,1)} %stack.20), calls=%async_computation | async-start | bytes 8388608 | tf_op jit(solution)/shard_map/all_to_all | solution.py:173
  28.8 11.6 %convert_reduce_fusion = (bf16[1536,128]{1,0:T(8,128)(2,1)S(1)}, bf16[1536]{0:T(1024)(128)(2,1)S(1)}) fusion(s32[128,8]{0,1:T(8,128)S(1)} %convert_add_fusion, f32[128,8]{0,1:T(8,128)S(1)} %fusion.55), kind=kLoop, calls=%fused_computation.5 | loop fusion | flops 7666176 | bytes 404480 | tf_op jit(solution)/shard_map/reduce_sum | solution.py:78
  44.1 5.8 %copy.131 = bf16[1536,1152]{1,0:T(8,128)(2,1)} copy(bf16[1536,1152]{0,1:T(8,128)(2,1)} %fusion.6) | data formatting | bytes 7077888 | tf_op jit(solution)/shard_map/concatenate | solution.py:82
  49.9 6.5 %reshape.416 = bf16[128,12,1152]{2,1,0:T(8,128)(2,1)} reshape(bf16[1536,1152]{1,0:T(8,128)(2,1)} %copy.131) | data formatting | bytes 7077888 | tf_op jit(solution)/shard_map/reshape | solution.py:92
  56.4 85.3 %all-to-all-done = bf16[64,1024,32]{1,2,0:T(8,128)(2,1)} async-done(((bf16[64,1024,32]{1,2,0:T(8,128)(2,1)}), bf16[64,1024,32]{1,2,0:T(8,128)(2,1)}, u32[]{:S(2)}, u32[]{:S(2)}) %all-to-all-start) | async-done | bytes 4194336 | tf_op jit(solution)/shard_map/all_to_all | solution.py:173
  141.7 36.6 %all-to-all-start.1 = ((bf16[128,12,1152]{2,1,0:T(8,128)(2,1)}), bf16[128,12,1152]{2,1,0:T(8,128)(2,1)}, u32[]{:S(2)}, u32[]{:S(2)}) async-start(bf16[128,12,1152]{2,1,0:T(8,128)(2,1)} %reshape.416), calls=%async_computation.1 | async-start | bytes 9437184 | tf_op jit(solution)/shard_map/all_to_all | solution.py:91
  190.4 4.3 collective-permute-start.4
  194.7 97.9 %all-to-all-done.1 = bf16[128,12,1152]{2,1,0:T(8,128)(2,1)} async-done(((bf16[128,12,1152]{2,1,0:T(8,128)(2,1)}), bf16[128,12,1152]{2,1,0:T(8,128)(2,1)}, u32[]{:S(2)}, u32[]{:S(2)}) %all-to-all-start.1) | async-done | bytes 3538976 | tf_op jit(solution)/shard_map/all_to_all | solution.py:91
  292.7 6.6 %reshape.417 = bf16[1536,1152]{1,0:T(8,128)(2,1)} reshape(bf16[128,12,1152]{2,1,0:T(8,128)(2,1)} %all-to-all-done.1) | data formatting | bytes 7077888 | tf_op jit(solution)/shard_map/reshape | solution.py:97
  301.2 6.1 %collective-permute-start.6 = (bf16[2,128,1,128]{3,1,2,0:T(8,128)(2,1)S(1)}, bf16[2,128,1,128]{3,1,2,0:T(8,128)(2,1)S(1)}, u32[]{:S(2)}, u32[]{:S(2)}) collective-permute-start(bf16[2,128,1,128]{3,1,2,0:T(8,128)(2,1)S(1)} %pad_maximum_fusion.3), channel_id=1, source_target_pairs={{0,24},{4,28},{8,32},{12,36},{16,40},{20,44},{24,48},{28,52},{32,5... | collective-permute-start | bytes 196616 | tf_op jit(solution)/shard_map/ppermute | solution.py:14
  307.3 5.3 %collective-permute-start.7 = (bf16[2,128,1,128]{3,1,2,0:T(8,128)(2,1)S(1)}, bf16[2,128,1,128]{3,1,2,0:T(8,128)(2,1)S(1)}, u32[]{:S(2)}, u32[]{:S(2)}) collective-permute-start(bf16[2,128,1,128]{3,1,2,0:T(8,128)(2,1)S(1)} %pad_maximum_fusion.3), channel_id=1, source_target_pairs={{0,28},{4,32},{8,36},{12,40},{16,44},{20,48},{24,52},{28,56},{32,6... | collective-permute-start | bytes 196616 | tf_op jit(solution)/shard_map/ppermute | solution.py:14
  312.6 7.7 %pad_maximum_fusion = bf16[1024,4096]{0,1:T(8,128)(2,1)} fusion(bf16[1024,2048]{0,1:T(8,128)(2,1)} %collective-permute-done, bf16[1024,2048]{0,1:T(8,128)(2,1)} %bitcast.1), kind=kLoop, calls=%fused_computation.1 | loop fusion | flops 16777216 | bytes 16777216 | tf_op jit(solution)/shard_map/concatenate | solution.py:176
  320.4 6.1 %fusion.9 = bf16[768,1536]{0,1:T(8,128)(2,1)} fusion(bf16[1536,1152]{1,0:T(8,128)(2,1)} %reshape.417, bf16[1,768,1024]{2,1,0:T(8,128)(2,1)S(1)} %copy-done), kind=kOutput, calls=%fused_computation.21 | convolution fusion | flops 2417098752 | bytes 7077888 | tf_op jit(solution)/shard_map/dot_general | solution.py:105
  326.6 4.4 copy.155
  334.1 36.1 %reduce-scatter.4.cloned.1.call-done = bf16[192,1536]{1,0:T(8,128)(2,1)} async-done(((bf16[768,1536]{1,0:T(8,128)(2,1)}), bf16[192,1536]{1,0:T(8,128)(2,1)}) %reduce-scatter.4.cloned.1.call-update) | async-done | bytes 589840
  374.0 12.9 %psum.7 = f32[128,1,12]{2,0,1:T(8,128)} all-reduce(f32[128,1,12]{2,0,1:T(8,128)S(1)} %all_to_all.14), channel_id=1, replica_groups=mesh['chip'=64,'core'=2,'head'=4] {'head'}, use_global_device_ids=true, to_apply=%region_9.0 | all-reduce | flops 1536 | bytes 12288 | tf_op jit(solution)/shard_map/psum | solution.py:122
  386.9 18.3 %all-to-all-start.2 = ((f32[128,1,12]{2,1,0:T(1,128)}), f32[128,1,12]{2,1,0:T(1,128)S(1)}, u32[]{:S(2)}, u32[]{:S(2)}) async-start(f32[128,1,12]{2,1,0:T(1,128)} %bitcast.13), calls=%async_computation.2 | async-start | bytes 131072 | tf_op jit(solution)/shard_map/all_to_all | solution.py:123
  405.6 7.9 %all-to-all-done.2 = f32[128,1,12]{2,1,0:T(1,128)S(1)} async-done(((f32[128,1,12]{2,1,0:T(1,128)}), f32[128,1,12]{2,1,0:T(1,128)S(1)}, u32[]{:S(2)}, u32[]{:S(2)}) %all-to-all-start.2) | async-done | bytes 6176 | tf_op jit(solution)/shard_map/all_to_all | solution.py:123
  414.9 6.2 %gather_fusion = f32[1024]{0:T(1024)S(1)} fusion(f32[1536]{0:T(1024)S(1)} %reshape.418, s32[1024]{0:T(1024)S(1)} %broadcast_clamp_fusion), kind=kCustom, calls=%fused_computation | custom fusion | bytes 12288 | tf_op jit(solution)/shard_map/jit(_take)/gather | solution.py:126
  427.0 17.6 %all-gather.2.cloned.1.call-done = bf16[128,4096]{1,0:T(8,128)(2,1)} async-done(((bf16[128,1024]{1,0:T(8,128)(2,1)}), bf16[128,4096]{1,0:T(8,128)(2,1)}) %all-gather.2.cloned.1.call-update) | async-done | bytes 1048592 | tf_op jit(solution)/shard_map/all_gather | solution.py:131
  446.3 4.8 convolution_convert_fusion.2
  465.8 9.3 %collective-permute-start.14 = (bf16[2,128,1,128]{3,1,2,0:T(8,128)(2,1)}, bf16[2,128,1,128]{3,1,2,0:T(8,128)(2,1)}, u32[]{:S(2)}, u32[]{:S(2)}) collective-permute-start(bf16[2,128,1,128]{3,1,2,0:T(8,128)(2,1)} %get-tuple-element.82), channel_id=1, source_target_pairs={{28,0},{32,4},{36,8},{40,12},{44,16},{48,20},{52,24},{56,28},{60,3... | collective-permute-start | bytes 196616 | tf_op jit(solution)/shard_map/ppermute | solution.py:14
  481.0 5.2 %collective-permute-start.12 = (bf16[2,128,1,128]{3,1,0,2:T(8,128)(2,1)S(1)}, bf16[2,128,1,128]{3,1,0,2:T(8,128)(2,1)S(1)}, u32[]{:S(2)}, u32[]{:S(2)}) collective-permute-start(bf16[2,128,1,128]{3,1,0,2:T(8,128)(2,1)S(1)} %get-tuple-element.84), channel_id=1, source_target_pairs={{20,0},{24,4},{28,8},{32,12},{36,16},{40,20},{44,24},{48,28},{52,3... | collective-permute-start | bytes 196616 | tf_op jit(solution)/shard_map/ppermute | solution.py:14
  489.8 4.4 collective-permute-start.10
  (168 shorter events, 72.3 us)
Async XLA Ops:
  7.2 313.3 %copy-start = (bf16[1,768,1024]{2,1,0:T(8,128)(2,1)S(1)}, bf16[1,768,1024]{2,1,0:T(8,128)(2,1)}, u32[]{:S(2)}) copy-start(bf16[1,768,1024]{2,1,0:T(8,128)(2,1)} %param.19) | copy-start | bytes 4718596
  10.7 131.0 %all-to-all-start = ((bf16[64,1024,32]{1,2,0:T(8,128)(2,1)}), bf16[64,1024,32]{1,2,0:T(8,128)(2,1)}, u32[]{:S(2)}, u32[]{:S(2)}) async-start(bf16[64,1024,32]{1,2,0:T(8,128)(2,1)} %stack.20), calls=%async_computation | async-start | bytes 8388608 | tf_op jit(solution)/shard_map/all_to_all | solution.py:173
  56.4 124.2 %copy-start.27 = (bf16[128,1,128]{2,0,1:T(8,128)(2,1)S(1)}, bf16[128,1,128]{2,0,1:T(8,128)(2,1)}, u32[]{:S(2)}) copy-start(bf16[128,1,128]{2,0,1:T(8,128)(2,1)} %param.24) | copy-start | bytes 98308
  56.4 124.2 %copy-start.28 = (bf16[128,1,128]{2,0,1:T(8,128)(2,1)S(1)}, bf16[128,1,128]{2,0,1:T(8,128)(2,1)}, u32[]{:S(2)}) copy-start(bf16[128,1,128]{2,0,1:T(8,128)(2,1)} %param.23) | copy-start | bytes 98308
  141.7 151.0 %all-to-all-start.1 = ((bf16[128,12,1152]{2,1,0:T(8,128)(2,1)}), bf16[128,12,1152]{2,1,0:T(8,128)(2,1)}, u32[]{:S(2)}, u32[]{:S(2)}) async-start(bf16[128,12,1152]{2,1,0:T(8,128)(2,1)} %reshape.416), calls=%async_computation.1 | async-start | bytes 9437184 | tf_op jit(solution)/shard_map/all_to_all | solution.py:91
  178.3 191.8 %reduce-scatter.4.cloned.1.call-start = ((), (), s32[]{:S(2)}) async-start(), calls=%async_computation.5 | async-start | bytes 2949120
  178.4 129.0 %collective-permute-start = (bf16[1024,2048]{0,1:T(8,128)(2,1)}, bf16[1024,2048]{0,1:T(8,128)(2,1)}, u32[]{:S(2)}, u32[]{:S(2)}) collective-permute-start(bf16[1024,2048]{0,1:T(8,128)(2,1)} %bitcast.1), channel_id=1, source_target_pairs={{0,4},{4,0},{1,5},{5,1},{2,6},{6,2},{3,7},{7,3},{8,12},{12,8},{9,1... | collective-permute-start | bytes 12582920 | tf_op jit(solution)/shard_map/ppermute | solution.py:175
  180.7 118.6 %collective-permute-start.1 = (bf16[2,128,1,128]{3,1,2,0:T(8,128)(2,1)S(1)}, bf16[2,128,1,128]{3,1,2,0:T(8,128)(2,1)S(1)}, u32[]{:S(2)}, u32[]{:S(2)}) collective-permute-start(bf16[2,128,1,128]{3,1,2,0:T(8,128)(2,1)S(1)} %pad_maximum_fusion.3), channel_id=1, source_target_pairs={{0,4},{4,8},{8,12},{12,16},{16,20},{20,24},{24,28},{28,32},{32,36}... | collective-permute-start | bytes 196616 | tf_op jit(solution)/shard_map/ppermute | solution.py:14
  183.8 117.4 %collective-permute-start.2 = (bf16[2,128,1,128]{3,1,2,0:T(8,128)(2,1)S(1)}, bf16[2,128,1,128]{3,1,2,0:T(8,128)(2,1)S(1)}, u32[]{:S(2)}, u32[]{:S(2)}) collective-permute-start(bf16[2,128,1,128]{3,1,2,0:T(8,128)(2,1)S(1)} %pad_maximum_fusion.3), channel_id=1, source_target_pairs={{0,8},{4,12},{8,16},{12,20},{16,24},{20,28},{24,32},{28,36},{32,40... | collective-permute-start | bytes 196616 | tf_op jit(solution)/shard_map/ppermute | solution.py:14
  186.9 133.4 %collective-permute-start.3 = (bf16[2,128,1,128]{3,1,2,0:T(8,128)(2,1)S(1)}, bf16[2,128,1,128]{3,1,2,0:T(8,128)(2,1)S(1)}, u32[]{:S(2)}, u32[]{:S(2)}) collective-permute-start(bf16[2,128,1,128]{3,1,2,0:T(8,128)(2,1)S(1)} %pad_maximum_fusion.3), channel_id=1, source_target_pairs={{0,12},{4,16},{8,20},{12,24},{16,28},{20,32},{24,36},{28,40},{32,4... | collective-permute-start | bytes 196616 | tf_op jit(solution)/shard_map/ppermute | solution.py:14
  190.4 130.0 %collective-permute-start.4 = (bf16[2,128,1,128]{3,1,2,0:T(8,128)(2,1)S(1)}, bf16[2,128,1,128]{3,1,2,0:T(8,128)(2,1)S(1)}, u32[]{:S(2)}, u32[]{:S(2)}) collective-permute-start(bf16[2,128,1,128]{3,1,2,0:T(8,128)(2,1)S(1)} %pad_maximum_fusion.3), channel_id=1, source_target_pairs={{0,16},{4,20},{8,24},{12,28},{16,32},{20,36},{24,40},{28,44},{32,4... | collective-permute-start | bytes 196616 | tf_op jit(solution)/shard_map/ppermute | solution.py:14
  299.3 21.1 %collective-permute-start.5 = (bf16[2,128,1,128]{3,1,2,0:T(8,128)(2,1)S(1)}, bf16[2,128,1,128]{3,1,2,0:T(8,128)(2,1)S(1)}, u32[]{:S(2)}, u32[]{:S(2)}) collective-permute-start(bf16[2,128,1,128]{3,1,2,0:T(8,128)(2,1)S(1)} %pad_maximum_fusion.3), channel_id=1, source_target_pairs={{0,20},{4,24},{8,28},{12,32},{16,36},{20,40},{24,44},{28,48},{32,5... | collective-permute-start | bytes 196616 | tf_op jit(solution)/shard_map/ppermute | solution.py:14
  301.2 19.2 %collective-permute-start.6 = (bf16[2,128,1,128]{3,1,2,0:T(8,128)(2,1)S(1)}, bf16[2,128,1,128]{3,1,2,0:T(8,128)(2,1)S(1)}, u32[]{:S(2)}, u32[]{:S(2)}) collective-permute-start(bf16[2,128,1,128]{3,1,2,0:T(8,128)(2,1)S(1)} %pad_maximum_fusion.3), channel_id=1, source_target_pairs={{0,24},{4,28},{8,32},{12,36},{16,40},{20,44},{24,48},{28,52},{32,5... | collective-permute-start | bytes 196616 | tf_op jit(solution)/shard_map/ppermute | solution.py:14
  307.3 13.1 %collective-permute-start.7 = (bf16[2,128,1,128]{3,1,2,0:T(8,128)(2,1)S(1)}, bf16[2,128,1,128]{3,1,2,0:T(8,128)(2,1)S(1)}, u32[]{:S(2)}, u32[]{:S(2)}) collective-permute-start(bf16[2,128,1,128]{3,1,2,0:T(8,128)(2,1)S(1)} %pad_maximum_fusion.3), channel_id=1, source_target_pairs={{0,28},{4,32},{8,36},{12,40},{16,44},{20,48},{24,52},{28,56},{32,6... | collective-permute-start | bytes 196616 | tf_op jit(solution)/shard_map/ppermute | solution.py:14
  371.5 50.6 %copy-start.9 = (bf16[128,1024]{1,0:T(8,128)(2,1)S(1)}, bf16[128,1024]{1,0:T(8,128)(2,1)}, u32[]{:S(2)}) copy-start(bf16[128,1024]{1,0:T(8,128)(2,1)} %param.14) | copy-start | bytes 786436
  386.9 26.6 %all-to-all-start.2 = ((f32[128,1,12]{2,1,0:T(1,128)}), f32[128,1,12]{2,1,0:T(1,128)S(1)}, u32[]{:S(2)}, u32[]{:S(2)}) async-start(f32[128,1,12]{2,1,0:T(1,128)} %bitcast.13), calls=%async_computation.2 | async-start | bytes 131072 | tf_op jit(solution)/shard_map/all_to_all | solution.py:123
  405.3 39.3 %all-gather.2.cloned.1.call-start = ((), (), s32[]{:S(2)}) async-start(), calls=%async_computation.4 | async-start | bytes 1310720 | tf_op jit(solution)/shard_map/all_gather | solution.py:131
  465.8 28.4 %collective-permute-start.14 = (bf16[2,128,1,128]{3,1,2,0:T(8,128)(2,1)}, bf16[2,128,1,128]{3,1,2,0:T(8,128)(2,1)}, u32[]{:S(2)}, u32[]{:S(2)}) collective-permute-start(bf16[2,128,1,128]{3,1,2,0:T(8,128)(2,1)} %get-tuple-element.82), channel_id=1, source_target_pairs={{28,0},{32,4},{36,8},{40,12},{44,16},{48,20},{52,24},{56,28},{60,3... | collective-permute-start | bytes 196616 | tf_op jit(solution)/shard_map/ppermute | solution.py:14
  475.1 21.1 %collective-permute-start.13 = (bf16[2,128,1,128]{3,1,0,2:T(8,128)(2,1)S(1)}, bf16[2,128,1,128]{3,1,0,2:T(8,128)(2,1)}, u32[]{:S(2)}, u32[]{:S(2)}) collective-permute-start(bf16[2,128,1,128]{3,1,0,2:T(8,128)(2,1)S(1)} %get-tuple-element.83), channel_id=1, source_target_pairs={{24,0},{28,4},{32,8},{36,12},{40,16},{44,20},{48,24},{52,28},{56,3... | collective-permute-start | bytes 196616 | tf_op jit(solution)/shard_map/ppermute | solution.py:14
  481.0 20.5 %collective-permute-start.12 = (bf16[2,128,1,128]{3,1,0,2:T(8,128)(2,1)S(1)}, bf16[2,128,1,128]{3,1,0,2:T(8,128)(2,1)S(1)}, u32[]{:S(2)}, u32[]{:S(2)}) collective-permute-start(bf16[2,128,1,128]{3,1,0,2:T(8,128)(2,1)S(1)} %get-tuple-element.84), channel_id=1, source_target_pairs={{20,0},{24,4},{28,8},{32,12},{36,16},{40,20},{44,24},{48,28},{52,3... | collective-permute-start | bytes 196616 | tf_op jit(solution)/shard_map/ppermute | solution.py:14
  486.1 15.3 %collective-permute-start.11 = (bf16[2,128,1,128]{3,1,0,2:T(8,128)(2,1)S(1)}, bf16[2,128,1,128]{3,1,0,2:T(8,128)(2,1)S(1)}, u32[]{:S(2)}, u32[]{:S(2)}) collective-permute-start(bf16[2,128,1,128]{3,1,0,2:T(8,128)(2,1)S(1)} %get-tuple-element.85), channel_id=1, source_target_pairs={{16,0},{20,4},{24,8},{28,12},{32,16},{36,20},{40,24},{44,28},{48,3... | collective-permute-start | bytes 196616 | tf_op jit(solution)/shard_map/ppermute | solution.py:14
  489.8 11.7 %collective-permute-start.10 = (bf16[2,128,1,128]{3,1,0,2:T(8,128)(2,1)S(1)}, bf16[2,128,1,128]{3,1,0,2:T(8,128)(2,1)S(1)}, u32[]{:S(2)}, u32[]{:S(2)}) collective-permute-start(bf16[2,128,1,128]{3,1,0,2:T(8,128)(2,1)S(1)} %get-tuple-element.86), channel_id=1, source_target_pairs={{12,0},{16,4},{20,8},{24,12},{28,16},{32,20},{36,24},{40,28},{44,3... | collective-permute-start | bytes 196616 | tf_op jit(solution)/shard_map/ppermute | solution.py:14
  494.2 7.3 %collective-permute-start.9 = (bf16[2,128,1,128]{3,1,0,2:T(8,128)(2,1)S(1)}, bf16[2,128,1,128]{3,1,0,2:T(8,128)(2,1)S(1)}, u32[]{:S(2)}, u32[]{:S(2)}) collective-permute-start(bf16[2,128,1,128]{3,1,0,2:T(8,128)(2,1)S(1)} %get-tuple-element.87), channel_id=1, source_target_pairs={{8,0},{12,4},{16,8},{20,12},{24,16},{28,20},{32,24},{36,28},{40,32... | collective-permute-start | bytes 196616 | tf_op jit(solution)/shard_map/ppermute | solution.py:14
  496.2 5.6 %collective-permute-start.8 = (bf16[2,128,1,128]{3,1,0,2:T(8,128)(2,1)S(1)}, bf16[2,128,1,128]{3,1,0,2:T(8,128)(2,1)S(1)}, u32[]{:S(2)}, u32[]{:S(2)}) collective-permute-start(bf16[2,128,1,128]{3,1,0,2:T(8,128)(2,1)S(1)} %get-tuple-element.81), channel_id=1, source_target_pairs={{4,0},{8,4},{12,8},{16,12},{20,16},{24,20},{28,24},{32,28},{36,32}... | collective-permute-start | bytes 196616 | tf_op jit(solution)/shard_map/ppermute | solution.py:14
  (29 other events, 726.5 us)
Sparse Core Ops, SparseCore 0:
  331.1 38.9 reduce-scatter.3
  423.3 21.2 all-gather.1
